TPU v7x, 32 devices: a whole 2x2x4 slice. The times are simulated.
32 devices in a mesh: row: 8 (over z, y), col: 4 (over x, core).
Axes of the slice: x: 2, y: 2, z: 4, core: 2. Of those that a mesh axis runs over, the one named last changes fastest.
Arguments:
- tokens: bfloat16 [1024, 4096], P('row'), may hold values from -6 to 6
- in_weight: bfloat16 [4096, 8192], P('row', 'col'), may hold values from -0.09375 to 0.09375
- gate_branch: bfloat16 [1024, 8192], P('row', 'col'), may hold values from -6 to 6
- conv_weight: float32 [4, 8192], P(None, 'col'), may hold values from -3 to 3
- out_weight: bfloat16 [8192, 4096], P('col'), may hold values from -0.0625 to 0.0625
- target: bfloat16 [1024, 4096], P('row'), may hold values from -6 to 6
- lang_ids: int32 [1024], P('row'), may hold values from 0 to 31
- lang_weight: float32 [32], replicated, may hold values from 0.25 to 4
- doc_pos: int32 [1024], P('row'), may hold values from 0 to 127, as said below
Outputs:
- block_out: bfloat16 [1024, 4096], P('row', 'col')
- grad_tokens: bfloat16 [1024, 4096], P('row', 'col')
- grad_gate: bfloat16 [1024, 8192], P('row', 'col')
Inputs may be any that keep to these rules, and one draw needn't show every extreme that they name: doc_pos is 0 at the first token and at every document's first token, and otherwise one more than the previous token's; no document is longer than 128 tokens and one is exactly 128 tokens long; apart from token 0, no document begins within the first 4 tokens of an aligned block of 128 tokens.
All inputs are finite; a program needn't handle non-finite values.
Results may differ from a plain program's by a relative error of at most 0.022.
Values may be sent and summed in bfloat16 or wider, within the bound.
No kernel may reach another device: no remote copies, remote signals or barrier semaphores. Data moves between devices by JAX's collectives and lax.ppermute only.
A program may use at most 128 MiB of HBM per device.

v0:
```python
import jax
import jax.numpy as jnp
from jax import lax
from jax.sharding import PartitionSpec as P

CONV = 4
LANGS = 32


def passed_along(value, axis, steps):
    count = lax.axis_size(axis)
    first, last = (max(0, -steps), min(count, count - steps))
    return lax.ppermute(value, axis, [(source, source + steps) for source in range(first, last)])


def silu_grad(argument):
    sigmoid_v = jax.nn.sigmoid(argument)
    return sigmoid_v * (1.0 + argument * (1.0 - sigmoid_v))


def shards(
    tokens, in_weight, gate_branch, conv_weight, out_weight, target, lang_ids, lang_weight, doc_pos
):
    row_count = tokens.shape[0]
    inner_width = gate_branch.shape[1]
    margin = CONV - 1
    moves_tokens = row_count * lax.axis_size("row") < tokens.shape[1]
    if moves_tokens:
        token_cols = lax.all_to_all(tokens, "row", 1, 0, tiled=True)
        part_x = jnp.dot(token_cols, in_weight, preferred_element_type=jnp.float32)
        inner_x = lax.psum_scatter(
            part_x.astype(jnp.bfloat16), "row", scatter_dimension=0, tiled=True
        )
    else:
        full_in = lax.all_gather(in_weight, "row", axis=0, tiled=True)
        inner_x = jnp.dot(tokens, full_in, preferred_element_type=jnp.float32).astype(jnp.bfloat16)
    from_prev = passed_along(inner_x[row_count - margin :], "row", 1)
    extended = jnp.concatenate([from_prev, inner_x], axis=0).astype(jnp.float32)
    conv_sum = jnp.zeros((row_count, inner_width), jnp.float32)
    for offset in range(CONV):
        keep_mask = (doc_pos >= offset).astype(jnp.float32)[:, None]
        conv_sum = (
            conv_sum
            + conv_weight[offset][None, :]
            * extended[margin - offset : margin - offset + row_count]
            * keep_mask
        )
    gate_value = gate_branch.astype(jnp.float32)
    gate_act = jax.nn.silu(gate_value)
    conv_act = jax.nn.silu(conv_sum)
    mixed = (conv_act * gate_act).astype(jnp.bfloat16)
    partial_value = jnp.dot(mixed, out_weight, preferred_element_type=jnp.float32)
    columns = tokens.shape[1] // lax.axis_size("col")
    col_start = lax.axis_index("col") * columns
    lang_table = (lang_ids[:, None] == jnp.arange(LANGS, dtype=jnp.int32)[None, :]).astype(
        jnp.float32
    )
    token_weight = jnp.sum(lang_table * lang_weight[None, :], axis=1)[:, None]
    out_total = lax.psum(partial_value.astype(jnp.bfloat16), "col").astype(jnp.float32)
    out_block = lax.dynamic_slice_in_dim(out_total, col_start, columns, 1)
    residual_grad = (token_weight * (out_total - target.astype(jnp.float32))).astype(jnp.bfloat16)
    grad_mixed = lax.dot_general(
        residual_grad, out_weight, (((1,), (1,)), ((), ())), preferred_element_type=jnp.float32
    )
    grad_conv = grad_mixed * gate_act * silu_grad(conv_sum)
    grad_gate = (grad_mixed * conv_act * silu_grad(gate_value)).astype(jnp.bfloat16)
    local_grad = conv_weight[0][None, :] * grad_conv
    spill_over = jnp.zeros((margin, inner_width), jnp.float32)
    for offset in range(1, CONV):
        masked = (
            conv_weight[offset][None, :]
            * grad_conv
            * (doc_pos >= offset).astype(jnp.float32)[:, None]
        )
        local_grad = local_grad + jnp.concatenate(
            [masked[offset:], jnp.zeros((offset, inner_width), jnp.float32)], axis=0
        )
        spill_over = spill_over + jnp.concatenate(
            [jnp.zeros((margin - offset, inner_width), jnp.float32), masked[:offset]], axis=0
        )
    from_next = passed_along(spill_over, "row", -1)
    grad_x = (
        local_grad
        + jnp.concatenate(
            [jnp.zeros((row_count - margin, inner_width), jnp.float32), from_next], axis=0
        )
    ).astype(jnp.bfloat16)
    if moves_tokens:
        grad_x_all = lax.all_gather(grad_x, "row", axis=0, tiled=True)
        grad_cols = lax.dot_general(
            grad_x_all, in_weight, (((1,), (1,)), ((), ())), preferred_element_type=jnp.float32
        )
        partial_grad = lax.all_to_all(grad_cols.astype(jnp.bfloat16), "row", 0, 1, tiled=True)
    else:
        partial_grad = lax.dot_general(
            grad_x, full_in, (((1,), (1,)), ((), ())), preferred_element_type=jnp.float32
        )
    grad_tokens = lax.psum_scatter(
        partial_grad.astype(jnp.bfloat16), "col", scatter_dimension=1, tiled=True
    )
    return (out_block.astype(jnp.bfloat16), grad_tokens, grad_gate)


def solution(mesh):
    in_specs = (
        P("row", None),
        P("row", "col"),
        P("row", "col"),
        P(None, "col"),
        P("col", None),
        P("row", None),
        P("row"),
        P(),
        P("row"),
    )
    out_specs = (P("row", "col"), P("row", "col"), P("row", "col"))
    return jax.shard_map(shards, mesh=mesh, in_specs=in_specs, out_specs=out_specs, check_vma=False)
```

profile of v0, /device:TPU:0, one launch (start us, length us, event | category | flops | bytes accessed | tf_op | source)
XLA Modules:
  0.0 352.7 jit_solution(13760163877622993587)
XLA Ops:
  7.2 2.4 copy.17
  9.6 33.0 %all_to_all.38 = bf16[128,8,512]{0,2,1:T(8,128)(2,1)S(1)} all-to-all(bf16[128,8,512]{0,2,1:T(8,128)(2,1)} %bitcast.20), channel_id=1, replica_groups=mesh['row'=8,'col'=4] {'row'}, dimensions={1} | all-to-all | bytes 2097152 | tf_op jit(solution)/shard_map/all_to_all | solution.py:29
  42.7 1.3 copy.18
  44.0 5.5 %convolution_convert_fusion.1 = bf16[1024,2048]{1,0:T(8,128)(2,1)} fusion(bf16[1024,512]{1,0:T(8,128)(2,1)} %bitcast.21, bf16[512,2048]{1,0:T(8,128)(2,1)S(1)} %copy-done), kind=kOutput, calls=%fused_computation.1 | convolution fusion | flops 2149580800 | bytes 7340032 | tf_op jit(solution)/shard_map/dot_general | solution.py:30
  49.5 0.0 all-reduce.8.cloned.1.call-start
  49.6 0.7 copy-done.3
  50.3 86.5 %reduce-scatter.3.cloned.1.call-done = bf16[128,2048]{1,0:T(8,128)(2,1)} async-done(((bf16[1024,2048]{1,0:T(8,128)(2,1)}), bf16[128,2048]{1,0:T(8,128)(2,1)}) %reduce-scatter.3.cloned.1.call-update) | async-done | bytes 524304 | tf_op jit(solution)/shard_map/reduce_scatter | solution.py:31
  136.8 0.8 slice.64
  137.6 3.4 collective-permute-start
  141.0 1.4 collective-permute-done
  142.4 1.2 maximum_convert_fusion
  143.6 0.7 fusion.9
  144.3 1.0 copy-done.2
  145.3 9.5 %convolution_convert_fusion = bf16[128,4096]{1,0:T(8,128)(2,1)} fusion(bf16[2048,4096]{1,0:T(8,128)(2,1)} %param.13, bf16[128,2048]{1,0:T(8,128)(2,1)S(1)} %copy-done.5, f32[128,2048]{1,0:T(8,128)S(1)} %fusion.9), kind=kOutput, calls=%fused_computation | convolution fusion | flops 2150891520 | bytes 19398656 | tf_op jit(solution)/shard_map/dot_general | solution.py:52
  154.9 0.1 select_reduce_fusion
  154.9 36.6 %all-reduce.8.cloned.1.call-done = bf16[128,4096]{1,0:T(8,128)(2,1)} async-done(((bf16[128,4096]{1,0:T(8,128)(2,1)}), bf16[128,4096]{1,0:T(8,128)(2,1)}) %all-reduce.8.cloned.1.call-update) | async-done | bytes 1048592 | tf_op jit(solution)/shard_map/psum | solution.py:59
  191.6 14.1 %multiply_multiply_fusion.2 = (f32[128,2048]{1,0:T(8,128)}, f32[128,2048]{1,0:T(8,128)S(1)}, bf16[128,2048]{1,0:T(8,128)(2,1)}) fusion(f32[128]{0:T(128)S(1)} %get-tuple-element.13, f32[2048]{0:T(1024)S(1)} %bitcast.30, f32[128,2048]{1,0:T(8,128)} %copy-done.2, bf16[128,2048]{1,0:T(8,128)(2,1)} %param.11, bf16[2048,4096]{1,0:T(8,128)(2,1)} %param.13, ...), kind=kOutput, calls=%fused_computation.29 | convolution fusion | flops 2156396544 | bytes 23077888 | tf_op jit(solution)/shard_map/dot_general | solution.py:62
  205.7 0.9 slice.72
  206.6 0.3 multiply_multiply_fusion.1
  206.9 1.5 collective-permute-start.1
  208.4 0.1 slice.69
  208.5 0.1 slice.70
  208.6 0.1 slice.71
  208.7 4.0 %collective-permute-done.1 = f32[3,2048]{1,0:T(4,128)S(1)} collective-permute-done((f32[3,2048]{1,0:T(4,128)S(1)}, f32[3,2048]{1,0:T(4,128)S(1)}, u32[]{:S(2)}, u32[]{:S(2)}) %collective-permute-start.1) | collective-permute-done | bytes 24608 | tf_op jit(solution)/shard_map/ppermute | solution.py:13
  212.7 1.2 add_convert_fusion
  213.9 0.0 reduce-scatter.5.cloned.1.call-start
  214.0 73.9 %all-gather.2.cloned.1.call-done = bf16[1024,2048]{1,0:T(8,128)(2,1)} async-done(((bf16[128,2048]{1,0:T(8,128)(2,1)}), bf16[1024,2048]{1,0:T(8,128)(2,1)}) %all-gather.2.cloned.1.call-update) | async-done | bytes 4194320 | tf_op jit(solution)/shard_map/all_gather | solution.py:89
  287.9 4.5 %convolution_convert_fusion.2 = bf16[1024,512]{1,0:T(8,128)(2,1)S(1)} fusion(bf16[1024,2048]{1,0:T(8,128)(2,1)} %all-gather.2.cloned.1.call-done, bf16[512,2048]{1,0:T(8,128)(2,1)S(1)} %copy-done), kind=kOutput, calls=%fused_computation.6 | convolution fusion | flops 2148007936 | bytes 7340032 | tf_op jit(solution)/shard_map/dot_general | solution.py:90
  292.4 28.5 %all_to_all.39 = bf16[8,128,512]{2,1,0:T(8,128)(2,1)S(1)} all-to-all(bf16[8,128,512]{2,1,0:T(8,128)(2,1)S(1)} %bitcast.22), channel_id=1, replica_groups=mesh['row'=8,'col'=4] {'row'}, dimensions={0} | all-to-all | bytes 2097152 | tf_op jit(solution)/shard_map/all_to_all | solution.py:93
  321.0 1.1 copy.20
  322.1 1.7 dynamic-slice_convert_fusion
  323.8 22.4 %reduce-scatter.5.cloned.1.call-done = bf16[128,1024]{1,0:T(8,128)(2,1)} async-done(((bf16[128,4096]{1,0:T(8,128)(2,1)}), bf16[128,1024]{1,0:T(8,128)(2,1)}) %reduce-scatter.5.cloned.1.call-update) | async-done | bytes 262160 | tf_op jit(solution)/shard_map/reduce_scatter | solution.py:98
  (24 shorter events, 0.2 us)
Async XLA Ops:
  7.2 36.8 %copy-start = (bf16[512,2048]{1,0:T(8,128)(2,1)S(1)}, bf16[512,2048]{1,0:T(8,128)(2,1)}, u32[]{:S(2)}) copy-start(bf16[512,2048]{1,0:T(8,128)(2,1)} %param.10) | copy-start | bytes 6291460
  7.2 129.6 %reduce-scatter.3.cloned.1.call-start = ((), (), s32[]{:S(2)}) async-start(), calls=%async_computation.4 | async-start | bytes 4718592 | tf_op jit(solution)/shard_map/reduce_scatter | solution.py:31
  49.5 0.8 copy-start.3
  49.5 91.4 %copy-start.4 = (s32[128]{0:T(128)S(1)}, s32[128]{0:T(128)}, u32[]{:S(2)}) copy-start(s32[128]{0:T(128)} %param.17) | copy-start | bytes 1540
  49.5 142.1 %all-reduce.8.cloned.1.call-start = ((), (), s32[]{:S(2)}) async-start(), calls=%async_computation.5 | async-start | bytes 2097152 | tf_op jit(solution)/shard_map/psum | solution.py:59
  137.6 4.8 %collective-permute-start = (bf16[3,2048]{1,0:T(4,128)(2,1)S(1)}, bf16[3,2048]{1,0:T(4,128)(2,1)S(1)}, u32[]{:S(2)}, u32[]{:S(2)}) collective-permute-start(bf16[3,2048]{1,0:T(4,128)(2,1)S(1)} %slice.64), channel_id=1, source_target_pairs={{0,4},{4,8},{8,12},{12,16},{16,20},{20,24},{24,28},{1,5},{5,9},{9,... | collective-permute-start | bytes 36872 | tf_op jit(solution)/shard_map/ppermute | solution.py:13
  143.6 1.7 copy-start.5
  144.3 1.0 copy-start.2
  145.3 9.5 %copy-start.6 = (f32[32]{0:T(128)S(1)}, f32[32]{0:T(128)}, u32[]{:S(2)}) copy-start(f32[32]{0:T(128)} %param.16) | copy-start | bytes 388
  145.3 9.5 %copy-start.7 = (s32[128]{0:T(128)S(1)}, s32[128]{0:T(128)}, u32[]{:S(2)}) copy-start(s32[128]{0:T(128)} %param.15) | copy-start | bytes 1540
  154.8 133.1 %all-gather.2.cloned.1.call-start = ((), (), s32[]{:S(2)}) async-start(), calls=%async_computation.6 | async-start | bytes 4718592 | tf_op jit(solution)/shard_map/all_gather | solution.py:89
  205.7 2.7 copy-start.1
  206.9 5.8 %collective-permute-start.1 = (f32[3,2048]{1,0:T(4,128)S(1)}, f32[3,2048]{1,0:T(4,128)S(1)}, u32[]{:S(2)}, u32[]{:S(2)}) collective-permute-start(f32[3,2048]{1,0:T(4,128)S(1)} %slice_add_fusion), channel_id=1, source_target_pairs={{4,0},{8,4},{12,8},{16,12},{20,16},{24,20},{28,24},{5,1},{9,5},{13... | collective-permute-start | bytes 73736 | tf_op jit(solution)/shard_map/ppermute | solution.py:13
  213.9 132.2 %reduce-scatter.5.cloned.1.call-start = ((), (), s32[]{:S(2)}) async-start(), calls=%async_computation.7 | async-start | bytes 1310720 | tf_op jit(solution)/shard_map/reduce_scatter | solution.py:98
Sparse Core Ops, SparseCore 0:
  49.7 87.0 reduce-scatter.2
  154.9 36.6 all-reduce.7
  214.1 73.7 all-gather.1
  322.2 23.9 reduce-scatter.4
where the time goes:
time: 353 us
  waiting for transfers between devices  225 us (64%)
  blocking collectives  61.6 us (17%)
  matrix products  33.6 us (10%)
  between operations  13.9 us (4%)
  local copies, waits for them, and re-layouts  10.2 us (3%)
  starting transfers between devices  5.03 us (1%)
    reduce_scatter x1, waiting for transfers between devices, shards(): lax.psum_scatter(part_x.astype(jnp.bfloat16), 'row', scatter_dimension=0,...  86.5 us
    all_gather x1, waiting for transfers between devices, shards(): grad_x_all = lax.all_gather(grad_x, 'row', axis=0, tiled=True)  73.9 us
    psum x1, waiting for transfers between devices, shards(): lax.psum(partial_value.astype(jnp.bfloat16), 'col').astype(jnp.float32)  36.6 us
    all_to_all x1, blocking collectives, shards(): token_cols = lax.all_to_all(tokens, 'row', 1, 0, tiled=True)  33 us
    all_to_all x1, blocking collectives, shards(): lax.all_to_all(grad_cols.astype(jnp.bfloat16), 'row', 0, 1, tiled=True)  28.5 us
    reduce_scatter x1, waiting for transfers between devices, shards(): lax.psum_scatter(partial_grad.astype(jnp.bfloat16), 'col', scatter_dimens...  22.4 us
    dot_general x1, matrix products, shards(): lax.dot_general(residual_grad, out_weight, (((1,), (1,)), ((), ())), pref...  14.1 us
    dot_general x1, matrix products, shards(): jnp.dot(mixed, out_weight, preferred_element_type=jnp.float32)  9.46 us
  transfers between devices with their start and end apart: 6, of which 6 were waited for; matrix products, arithmetic and copies ran while one was open for 1% of the time, Pallas kernels for 0%

commit v1 on v0

--- a/solution.py
+++ b/solution.py
@@ -86,7 +86,14 @@
         )
     ).astype(jnp.bfloat16)
     if moves_tokens:
-        grad_x_all = lax.all_gather(grad_x, "row", axis=0, tiled=True)
+        ring = [grad_x]
+        for hop in range(7):
+            ring.append(lax.ppermute(ring[-1], "row", [(dev, (dev + 1) % 8) for dev in range(8)]))
+        grad_x_all = jnp.roll(
+            jnp.concatenate(ring[::-1], axis=0),
+            (lax.axis_index("row") + 1) * ring[0].shape[0],
+            axis=0,
+        )
         grad_cols = lax.dot_general(
             grad_x_all, in_weight, (((1,), (1,)), ((), ())), preferred_element_type=jnp.float32
         )

time: 353 us -> 374 us (1.059)
  waiting for transfers between devices: 225 us -> 240 us
  local copies, waits for them, and re-layouts: 10.2 us -> 22.8 us
  blocking collectives: 61.6 us -> 53.1 us
    ppermute x0 -> x7, waiting for transfers between devices: none -> 90.1 us  [shards(): lax.ppermute(ring[-1], 'row', [(dev, (dev + 1) % 8) for dev in range(8)])]
    all_gather x1 -> x0, waiting for transfers between devices: 73.9 us -> none  [shards(): grad_x_all = lax.all_gather(grad_x, 'row', axis=0, tiled=True)]
    unnamed x17 -> x48, local copies, waits for them, and re-layouts: 4.1 us -> 15.5 us
    all_to_all x1, blocking collectives: 28.5 us -> 20.1 us  [shards(): lax.all_to_all(grad_cols.astype(jnp.bfloat16), 'row', 0, 1, tiled=True)]
  transfers between devices with their start and end apart: 6 -> 12, of which waited for: 6 -> 12; matrix products, arithmetic and copies ran while one was open for 1% -> 1% of each run, Pallas kernels for 0% -> 0%
where the time goes in v1:
time: 374 us; the launch traced here: 373 us
  waiting for transfers between devices  240 us (64%)
  blocking collectives  53.1 us (14%)
  matrix products  31.4 us (8%)
  local copies, waits for them, and re-layouts  22.8 us (6%)
  between operations  14.1 us (4%)
  starting transfers between devices  7.4 us (2%)
  other arithmetic  3.87 us (1%)
    ppermute x7, waiting for transfers between devices, shards(): lax.ppermute(ring[-1], 'row', [(dev, (dev + 1) % 8) for dev in range(8)])  90.1 us
    reduce_scatter x1, waiting for transfers between devices, shards(): lax.psum_scatter(part_x.astype(jnp.bfloat16), 'row', scatter_dimension=0,...  87 us
    psum x1, waiting for transfers between devices, shards(): lax.psum(partial_value.astype(jnp.bfloat16), 'col').astype(jnp.float32)  36.6 us
    all_to_all x1, blocking collectives, shards(): token_cols = lax.all_to_all(tokens, 'row', 1, 0, tiled=True)  33 us
    reduce_scatter x1, waiting for transfers between devices, shards(): lax.psum_scatter(partial_grad.astype(jnp.bfloat16), 'col', scatter_dimens...  22.1 us
    all_to_all x1, blocking collectives, shards(): lax.all_to_all(grad_cols.astype(jnp.bfloat16), 'row', 0, 1, tiled=True)  20.1 us
    unnamed x48, local copies, waits for them, and re-layouts  15.5 us
    dot_general x1, matrix products, shards(): lax.dot_general(residual_grad, out_weight, (((1,), (1,)), ((), ())), pref...  14.1 us
  transfers between devices with their start and end apart: 12, of which 12 were waited for; matrix products, arithmetic and copies ran while one was open for 1% of the time, Pallas kernels for 0%

profile of v1, /device:TPU:0, one launch (start us, length us, event | category | flops | bytes accessed | tf_op | source)
XLA Modules:
  0.0 372.7 jit_solution(6157833853131735647)
XLA Ops:
  7.2 2.4 copy.17
  9.6 33.0 %all_to_all.38 = bf16[128,8,512]{0,2,1:T(8,128)(2,1)S(1)} all-to-all(bf16[128,8,512]{0,2,1:T(8,128)(2,1)} %bitcast.19), channel_id=1, replica_groups=mesh['row'=8,'col'=4] {'row'}, dimensions={1} | all-to-all | bytes 2097152 | tf_op jit(solution)/shard_map/all_to_all | solution.py:29
  42.7 1.3 copy.18
  44.0 5.5 %convolution_convert_fusion.1 = bf16[1024,2048]{1,0:T(8,128)(2,1)} fusion(bf16[1024,512]{1,0:T(8,128)(2,1)} %bitcast.21, bf16[512,2048]{1,0:T(8,128)(2,1)S(1)} %copy-done), kind=kOutput, calls=%fused_computation.3 | convolution fusion | flops 2149580800 | bytes 7340032 | tf_op jit(solution)/shard_map/dot_general | solution.py:30
  49.7 87.0 %reduce-scatter.3.cloned.1.call-done = bf16[128,2048]{1,0:T(8,128)(2,1)} async-done(((bf16[1024,2048]{1,0:T(8,128)(2,1)}), bf16[128,2048]{1,0:T(8,128)(2,1)}) %reduce-scatter.3.cloned.1.call-update) | async-done | bytes 524304 | tf_op jit(solution)/shard_map/reduce_scatter | solution.py:31
  137.4 3.4 collective-permute-start
  140.8 1.4 collective-permute-done
  142.2 1.2 maximum_convert_fusion
  145.1 9.4 %convolution_convert_fusion = bf16[128,4096]{1,0:T(8,128)(2,1)} fusion(bf16[2048,4096]{1,0:T(8,128)(2,1)} %param.13, bf16[128,2048]{1,0:T(8,128)(2,1)S(1)} %copy-done.13, f32[128,2048]{1,0:T(8,128)S(1)} %fusion.14), kind=kOutput, calls=%fused_computation | convolution fusion | flops 2150891520 | bytes 19398656 | tf_op jit(solution)/shard_map/dot_general | solution.py:52
  154.7 36.6 %all-reduce.8.cloned.1.call-done = bf16[128,4096]{1,0:T(8,128)(2,1)} async-done(((bf16[128,4096]{1,0:T(8,128)(2,1)}), bf16[128,4096]{1,0:T(8,128)(2,1)}) %all-reduce.8.cloned.1.call-update) | async-done | bytes 1048592 | tf_op jit(solution)/shard_map/psum | solution.py:59
  191.4 14.1 %multiply_multiply_fusion.2 = (f32[128,2048]{1,0:T(8,128)}, f32[128,2048]{1,0:T(8,128)S(1)}, bf16[128,2048]{1,0:T(8,128)(2,1)}) fusion(f32[128]{0:T(128)S(1)} %get-tuple-element.13, f32[2048]{0:T(1024)S(1)} %bitcast.29, f32[128,2048]{1,0:T(8,128)} %copy-done.10, bf16[128,2048]{1,0:T(8,128)(2,1)} %param.11, bf16[2048,4096]{1,0:T(8,128)(2,1)} %param.13, ...), kind=kOutput, calls=%fused_computation.31 | convolution fusion | flops 2156396544 | bytes 23077888 | tf_op jit(solution)/shard_map/dot_general | solution.py:62
  206.7 1.5 collective-permute-start.1
  208.1 1.3 slice.69
  209.6 2.8 collective-permute-done.1
  212.5 1.6 add_convert_fusion
  214.0 2.4 collective-permute-start.2
  216.5 12.6 %collective-permute-done.2 = bf16[128,2048]{1,0:T(8,128)(2,1)S(1)} collective-permute-done((bf16[128,2048]{1,0:T(8,128)(2,1)S(1)}, bf16[128,2048]{1,0:T(8,128)(2,1)S(1)}, u32[]{:S(2)}, u32[]{:S(2)}) %collective-permute-start.2) | collective-permute-done | bytes 524320 | tf_op jit(solution)/shard_map/ppermute | solution.py:91
  229.1 14.1 %collective-permute-done.3 = bf16[128,2048]{1,0:T(8,128)(2,1)S(1)} collective-permute-done((bf16[128,2048]{1,0:T(8,128)(2,1)S(1)}, bf16[128,2048]{1,0:T(8,128)(2,1)S(1)}, u32[]{:S(2)}, u32[]{:S(2)}) %collective-permute-start.3) | collective-permute-done | bytes 524320 | tf_op jit(solution)/shard_map/ppermute | solution.py:91
  244.0 13.1 %collective-permute-done.4 = bf16[128,2048]{1,0:T(8,128)(2,1)S(1)} collective-permute-done((bf16[128,2048]{1,0:T(8,128)(2,1)S(1)}, bf16[128,2048]{1,0:T(8,128)(2,1)S(1)}, u32[]{:S(2)}, u32[]{:S(2)}) %collective-permute-start.4) | collective-permute-done | bytes 524320 | tf_op jit(solution)/shard_map/ppermute | solution.py:91
  257.9 12.2 %collective-permute-done.5 = bf16[128,2048]{1,0:T(8,128)(2,1)S(1)} collective-permute-done((bf16[128,2048]{1,0:T(8,128)(2,1)S(1)}, bf16[128,2048]{1,0:T(8,128)(2,1)S(1)}, u32[]{:S(2)}, u32[]{:S(2)}) %collective-permute-start.5) | collective-permute-done | bytes 524320 | tf_op jit(solution)/shard_map/ppermute | solution.py:91
  270.9 12.1 %collective-permute-done.6 = bf16[128,2048]{1,0:T(8,128)(2,1)S(1)} collective-permute-done((bf16[128,2048]{1,0:T(8,128)(2,1)S(1)}, bf16[128,2048]{1,0:T(8,128)(2,1)S(1)}, u32[]{:S(2)}, u32[]{:S(2)}) %collective-permute-start.6) | collective-permute-done | bytes 524320 | tf_op jit(solution)/shard_map/ppermute | solution.py:91
  283.8 13.8 %collective-permute-done.7 = bf16[128,2048]{1,0:T(8,128)(2,1)} collective-permute-done((bf16[128,2048]{1,0:T(8,128)(2,1)S(1)}, bf16[128,2048]{1,0:T(8,128)(2,1)}, u32[]{:S(2)}, u32[]{:S(2)}) %collective-permute-start.7) | collective-permute-done | bytes 524320 | tf_op jit(solution)/shard_map/ppermute | solution.py:91
  297.6 12.2 %collective-permute-done.8 = bf16[128,2048]{1,0:T(8,128)(2,1)} collective-permute-done((bf16[128,2048]{1,0:T(8,128)(2,1)}, bf16[128,2048]{1,0:T(8,128)(2,1)}, u32[]{:S(2)}, u32[]{:S(2)}) %collective-permute-start.8) | collective-permute-done | bytes 524320 | tf_op jit(solution)/shard_map/ppermute | solution.py:91
  310.9 1.1 constant_dynamic-update-slice_fusion.14
  312.0 1.1 constant_dynamic-update-slice_fusion.13
  313.1 1.1 constant_dynamic-update-slice_fusion.12
  316.4 1.1 constant_dynamic-update-slice_fusion.7
  317.5 1.1 constant_dynamic-update-slice_fusion.6
  318.9 2.4 fusion.2
  321.3 20.1 %all_to_all.39 = bf16[8,128,512]{2,1,0:T(8,128)(2,1)S(1)} all-to-all(bf16[8,128,512]{2,1,0:T(8,128)(2,1)S(1)} %bitcast.20), channel_id=1, replica_groups=mesh['row'=8,'col'=4] {'row'}, dimensions={0} | all-to-all | bytes 2097152 | tf_op jit(solution)/shard_map/all_to_all | solution.py:100
  342.5 1.7 dynamic-slice_convert_fusion
  344.1 22.1 %reduce-scatter.5.cloned.1.call-done = bf16[128,1024]{1,0:T(8,128)(2,1)} async-done(((bf16[128,4096]{1,0:T(8,128)(2,1)}), bf16[128,1024]{1,0:T(8,128)(2,1)}) %reduce-scatter.5.cloned.1.call-update) | async-done | bytes 262160 | tf_op jit(solution)/shard_map/reduce_scatter | solution.py:105
  (67 shorter events, 12.0 us)
Async XLA Ops:
  7.2 36.8 %copy-start = (bf16[512,2048]{1,0:T(8,128)(2,1)S(1)}, bf16[512,2048]{1,0:T(8,128)(2,1)}, u32[]{:S(2)}) copy-start(bf16[512,2048]{1,0:T(8,128)(2,1)} %param.10) | copy-start | bytes 6291460
  7.2 129.5 %reduce-scatter.3.cloned.1.call-start = ((), (), s32[]{:S(2)}) async-start(), calls=%async_computation.4 | async-start | bytes 4718592 | tf_op jit(solution)/shard_map/reduce_scatter | solution.py:31
  44.0 5.6 %copy-start.11 = (f32[4,2048]{1,0:T(4,128)S(1)}, f32[4,2048]{1,0:T(4,128)}, u32[]{:S(2)}) copy-start(f32[4,2048]{1,0:T(4,128)} %param.12) | copy-start | bytes 98308
  44.0 96.8 %copy-start.12 = (s32[128]{0:T(128)S(1)}, s32[128]{0:T(128)}, u32[]{:S(2)}) copy-start(s32[128]{0:T(128)} %param.17) | copy-start | bytes 1540
  49.5 95.6 %copy-start.13 = (bf16[128,2048]{1,0:T(8,128)(2,1)S(1)}, bf16[128,2048]{1,0:T(8,128)(2,1)}, u32[]{:S(2)}) copy-start(bf16[128,2048]{1,0:T(8,128)(2,1)} %param.11) | copy-start | bytes 1572868
  49.6 141.8 %all-reduce.8.cloned.1.call-start = ((), (), s32[]{:S(2)}) async-start(), calls=%async_computation.5 | async-start | bytes 2097152 | tf_op jit(solution)/shard_map/psum | solution.py:59
  137.4 4.8 %collective-permute-start = (bf16[3,2048]{1,0:T(4,128)(2,1)S(1)}, bf16[3,2048]{1,0:T(4,128)(2,1)S(1)}, u32[]{:S(2)}, u32[]{:S(2)}) collective-permute-start(bf16[3,2048]{1,0:T(4,128)(2,1)S(1)} %slice.64), channel_id=1, source_target_pairs={{0,4},{4,8},{8,12},{12,16},{16,20},{20,24},{24,28},{1,5},{5,9},{9,... | collective-permute-start | bytes 36872 | tf_op jit(solution)/shard_map/ppermute | solution.py:13
  144.1 1.0 copy-start.10
  145.1 9.5 %copy-start.14 = (f32[32]{0:T(128)S(1)}, f32[32]{0:T(128)}, u32[]{:S(2)}) copy-start(f32[32]{0:T(128)} %param.16) | copy-start | bytes 388
  145.1 9.5 %copy-start.15 = (s32[128]{0:T(128)S(1)}, s32[128]{0:T(128)}, u32[]{:S(2)}) copy-start(s32[128]{0:T(128)} %param.15) | copy-start | bytes 1540
  154.6 211.6 %reduce-scatter.5.cloned.1.call-start = ((), (), s32[]{:S(2)}) async-start(), calls=%async_computation.6 | async-start | bytes 1310720 | tf_op jit(solution)/shard_map/reduce_scatter | solution.py:105
  205.4 4.2 %copy-start.1 = (f32[128,2048]{1,0:T(8,128)}, f32[128,2048]{1,0:T(8,128)S(1)}, u32[]{:S(2)}) copy-start(f32[128,2048]{1,0:T(8,128)S(1)} %get-tuple-element.4) | copy-start | bytes 3145732
  206.7 5.8 %collective-permute-start.1 = (f32[3,2048]{1,0:T(4,128)S(1)}, f32[3,2048]{1,0:T(4,128)S(1)}, u32[]{:S(2)}, u32[]{:S(2)}) collective-permute-start(f32[3,2048]{1,0:T(4,128)S(1)} %slice_add_fusion), channel_id=1, source_target_pairs={{4,0},{8,4},{12,8},{16,12},{20,16},{24,20},{28,24},{5,1},{9,5},{13... | collective-permute-start | bytes 73736 | tf_op jit(solution)/shard_map/ppermute | solution.py:13
  214.0 15.0 %collective-permute-start.2 = (bf16[128,2048]{1,0:T(8,128)(2,1)S(1)}, bf16[128,2048]{1,0:T(8,128)(2,1)S(1)}, u32[]{:S(2)}, u32[]{:S(2)}) collective-permute-start(bf16[128,2048]{1,0:T(8,128)(2,1)S(1)} %add_convert_fusion), channel_id=1, source_target_pairs={{0,4},{4,8},{8,12},{12,16},{16,20},{20,24},{24,28},{28,0},{1,5},{5... | collective-permute-start | bytes 1572872 | tf_op jit(solution)/shard_map/ppermute | solution.py:91
  229.1 14.1 %collective-permute-start.3 = (bf16[128,2048]{1,0:T(8,128)(2,1)S(1)}, bf16[128,2048]{1,0:T(8,128)(2,1)S(1)}, u32[]{:S(2)}, u32[]{:S(2)}) collective-permute-start(bf16[128,2048]{1,0:T(8,128)(2,1)S(1)} %collective-permute-done.2), channel_id=1, source_target_pairs={{0,4},{4,8},{8,12},{12,16},{16,20},{20,24},{24,28},{28,0},{1,5},{5... | collective-permute-start | bytes 1572872 | tf_op jit(solution)/shard_map/ppermute | solution.py:91
  243.1 0.8 copy-start.2
  244.0 13.1 %collective-permute-start.4 = (bf16[128,2048]{1,0:T(8,128)(2,1)S(1)}, bf16[128,2048]{1,0:T(8,128)(2,1)S(1)}, u32[]{:S(2)}, u32[]{:S(2)}) collective-permute-start(bf16[128,2048]{1,0:T(8,128)(2,1)S(1)} %collective-permute-done.3), channel_id=1, source_target_pairs={{0,4},{4,8},{8,12},{12,16},{16,20},{20,24},{24,28},{28,0},{1,5},{5... | collective-permute-start | bytes 1572872 | tf_op jit(solution)/shard_map/ppermute | solution.py:91
  257.1 0.8 copy-start.4
  257.9 12.2 %collective-permute-start.5 = (bf16[128,2048]{1,0:T(8,128)(2,1)S(1)}, bf16[128,2048]{1,0:T(8,128)(2,1)S(1)}, u32[]{:S(2)}, u32[]{:S(2)}) collective-permute-start(bf16[128,2048]{1,0:T(8,128)(2,1)S(1)} %collective-permute-done.4), channel_id=1, source_target_pairs={{0,4},{4,8},{8,12},{12,16},{16,20},{20,24},{24,28},{28,0},{1,5},{5... | collective-permute-start | bytes 1572872 | tf_op jit(solution)/shard_map/ppermute | solution.py:91
  270.1 0.8 copy-start.6
  270.9 12.1 %collective-permute-start.6 = (bf16[128,2048]{1,0:T(8,128)(2,1)S(1)}, bf16[128,2048]{1,0:T(8,128)(2,1)S(1)}, u32[]{:S(2)}, u32[]{:S(2)}) collective-permute-start(bf16[128,2048]{1,0:T(8,128)(2,1)S(1)} %collective-permute-done.5), channel_id=1, source_target_pairs={{0,4},{4,8},{8,12},{12,16},{16,20},{20,24},{24,28},{28,0},{1,5},{5... | collective-permute-start | bytes 1572872 | tf_op jit(solution)/shard_map/ppermute | solution.py:91
  283.0 0.8 copy-start.8
  283.8 13.8 %collective-permute-start.7 = (bf16[128,2048]{1,0:T(8,128)(2,1)S(1)}, bf16[128,2048]{1,0:T(8,128)(2,1)}, u32[]{:S(2)}, u32[]{:S(2)}) collective-permute-start(bf16[128,2048]{1,0:T(8,128)(2,1)S(1)} %collective-permute-done.6), channel_id=1, source_target_pairs={{0,4},{4,8},{8,12},{12,16},{16,20},{20,24},{24,28},{28,0},{1,5},{5... | collective-permute-start | bytes 1572872 | tf_op jit(solution)/shard_map/ppermute | solution.py:91
  297.6 12.2 %collective-permute-start.8 = (bf16[128,2048]{1,0:T(8,128)(2,1)}, bf16[128,2048]{1,0:T(8,128)(2,1)}, u32[]{:S(2)}, u32[]{:S(2)}) collective-permute-start(bf16[128,2048]{1,0:T(8,128)(2,1)} %collective-permute-done.7), channel_id=1, source_target_pairs={{0,4},{4,8},{8,12},{12,16},{16,20},{20,24},{24,28},{28,0},{1,5},{5... | collective-permute-start | bytes 1572872 | tf_op jit(solution)/shard_map/ppermute | solution.py:91
  297.6 21.0 %copy-start.9 = (bf16[128,2048]{1,0:T(8,128)(2,1)S(1)}, bf16[128,2048]{1,0:T(8,128)(2,1)}, u32[]{:S(2)}) copy-start(bf16[128,2048]{1,0:T(8,128)(2,1)} %copy-done.8) | copy-start | bytes 1572868
  297.6 21.1 %copy-start.7 = (bf16[128,2048]{1,0:T(8,128)(2,1)S(1)}, bf16[128,2048]{1,0:T(8,128)(2,1)}, u32[]{:S(2)}) copy-start(bf16[128,2048]{1,0:T(8,128)(2,1)} %copy-done.6) | copy-start | bytes 1572868
  297.6 21.1 %copy-start.5 = (bf16[128,2048]{1,0:T(8,128)(2,1)S(1)}, bf16[128,2048]{1,0:T(8,128)(2,1)}, u32[]{:S(2)}) copy-start(bf16[128,2048]{1,0:T(8,128)(2,1)} %copy-done.4) | copy-start | bytes 1572868
  297.6 21.2 %copy-start.3 = (bf16[128,2048]{1,0:T(8,128)(2,1)S(1)}, bf16[128,2048]{1,0:T(8,128)(2,1)}, u32[]{:S(2)}) copy-start(bf16[128,2048]{1,0:T(8,128)(2,1)} %copy-done.2) | copy-start | bytes 1572868
Sparse Core Ops, SparseCore 0:
  49.7 86.9 reduce-scatter.2
  154.7 36.6 all-reduce.7
  342.6 23.5 reduce-scatter.4
